TPU v7x, 32 devices: a whole 2x2x4 slice. The times are simulated.
32 devices in a mesh: groups: 2 (over y), ctx: 4 (over z), fsdp: 2 (over x), sub: 2 (over core).
Axes of the slice: x: 2, y: 2, z: 4, core: 2. Of those that a mesh axis runs over, the one named last changes fastest.
Arguments:
- layer_input: bfloat16 [4, 2048, 2304], P(('groups', 'fsdp'), ('ctx', 'sub')), parts along dimension 0, may hold values from -6 to 6
- query_heads: bfloat16 [4, 2048, 1024], P(('groups', 'fsdp'), ('ctx', 'sub')), parts along dimension 0, may hold values from -11 to 11
- key_heads: bfloat16 [4, 2048, 512], P(('groups', 'fsdp'), ('ctx', 'sub')), parts along dimension 0, may hold values from -11 to 11
- value_heads: bfloat16 [4, 2048, 512], P(('groups', 'fsdp'), ('ctx', 'sub')), parts along dimension 0, may hold values from -6 to 6
- grad_out: bfloat16 [4, 2048, 1024], P(('groups', 'fsdp'), ('ctx', 'sub')), parts along dimension 0, may hold values from -96 to 96
- doc_starts: int32 [4, 12], P(('groups', 'fsdp')), parts along dimension 0, may hold values from 0 to 2047, as said below
Outputs:
- grad_query: bfloat16 [4, 2048, 1024], P(('groups', 'fsdp'), ('ctx', 'sub')), parts along dimension 0
- grad_key: bfloat16 [4, 2048, 512], P(('groups', 'fsdp'), ('ctx', 'sub')), parts along dimension 0
- grad_value: bfloat16 [4, 2048, 512], P(('groups', 'fsdp'), ('ctx', 'sub')), parts along dimension 0
- grad_value_proj: float32 [4608, 512], P(('groups', 'fsdp')), parts along dimension 0
There are 2 independent parts, one for each index of `groups`. A program takes and returns all parts, laid end to end along the dimension named above; each array names one. Nothing has to cross between parts.
Inputs may be any that keep to these rules, and one draw needn't show every extreme that they name: `doc_starts`: each row holds the first positions of the 12 documents of one sequence in increasing order; the first is 0, every document has at least one token, and the longest has exactly 1024 tokens.
All inputs are finite; a program needn't handle non-finite values.
Results may differ from a plain program's by a relative error of at most 0.015.
Values may be sent and summed in bfloat16 or wider, within the bound.
No kernel may reach another device: no remote copies, remote signals or barrier semaphores. Data moves between devices by JAX's collectives and lax.ppermute only.
A program may use at most 64 MiB of HBM per device.

v0:
```python
import jax
import jax.numpy as jnp
from jax import lax
from jax.sharding import PartitionSpec as P

HEAD_DIM = 256
SPAN = 768


def passed_along(value, axis, steps):
    count = lax.axis_size(axis)
    first, last = (max(0, -steps), min(count, count - steps))
    return lax.ppermute(value, axis, [(source, source + steps) for source in range(first, last)])


def doc_start_of(starts, positions):
    covered = starts[None, :] <= positions[:, None]
    return jnp.max(jnp.where(covered, starts[None, :], 0), axis=1)


def attend_block(queries, key_block, value_block, grads, query_pos, key_pos, lowest):
    row_count = queries.shape[0]
    key_count = key_block.shape[0]
    groups = key_block.shape[1] // HEAD_DIM
    per_group = queries.shape[1] // key_block.shape[1]
    inv_root = HEAD_DIM ** (-0.5)
    query_four = queries.reshape(row_count, groups, per_group, HEAD_DIM)
    grad_four = grads.reshape(row_count, groups, per_group, HEAD_DIM)
    key_three = key_block.reshape(key_count, groups, HEAD_DIM)
    value_three = value_block.reshape(key_count, groups, HEAD_DIM)
    allowed = (key_pos[None, :] >= lowest[:, None]) & (key_pos[None, :] <= query_pos[:, None])

    def one_group(group):
        query_g = lax.dynamic_index_in_dim(query_four, group, 1, keepdims=False)
        grad_g = lax.dynamic_index_in_dim(grad_four, group, 1, keepdims=False)
        key_g = lax.dynamic_index_in_dim(key_three, group, 1, keepdims=False)
        value_g = lax.dynamic_index_in_dim(value_three, group, 1, keepdims=False)
        scores = (
            jnp.einsum("thd,kd->htk", query_g, key_g, preferred_element_type=jnp.float32) * inv_root
        )
        scores = jnp.where(allowed[None], scores, -1e30)
        largest = jnp.max(scores, axis=2, keepdims=True)
        raised = jnp.where(allowed[None], jnp.exp(scores - largest), 0.0)
        attn_probs = raised / jnp.sum(raised, axis=2, keepdims=True)
        grad_probs = jnp.einsum("thd,kd->htk", grad_g, value_g, preferred_element_type=jnp.float32)
        row_dot = jnp.sum(attn_probs * grad_probs, axis=2, keepdims=True)
        grad_scores = (attn_probs * (grad_probs - row_dot) * inv_root).astype(jnp.bfloat16)
        probs_low = attn_probs.astype(jnp.bfloat16)
        grad_q = jnp.einsum("htk,kd->thd", grad_scores, key_g, preferred_element_type=jnp.float32)
        grad_k = jnp.einsum("htk,thd->kd", grad_scores, query_g, preferred_element_type=jnp.float32)
        grad_v = jnp.einsum("htk,thd->kd", probs_low, grad_g, preferred_element_type=jnp.float32)
        return (grad_q, grad_k, grad_v)

    grad_q, grad_k, grad_v = lax.map(one_group, jnp.arange(groups, dtype=jnp.int32))
    grad_q = jnp.moveaxis(grad_q, 0, 1).reshape(row_count, -1)
    grad_k = jnp.moveaxis(grad_k, 0, 1).reshape(key_count, -1)
    grad_v = jnp.moveaxis(grad_v, 0, 1).reshape(key_count, -1)
    return (grad_q, grad_k, grad_v)


def body(layer_input, query_heads, key_heads, value_heads, grad_out, doc_starts):
    block_rows = query_heads.shape[1]
    window = min(SPAN, lax.axis_size(("ctx", "sub")) * block_rows // 2)
    reach_blocks = (window + block_rows - 2) // block_rows
    margin_rows = reach_blocks * block_rows
    key_count = margin_rows + block_rows
    first_row = lax.axis_index(("ctx", "sub")) * block_rows
    own_keys = key_heads[0]
    own_values = value_heads[0]
    arrived = []
    moving_k = own_keys
    moving_v = own_values
    for distance in range(reach_blocks):
        moving_k, moving_v = passed_along((moving_k, moving_v), ("ctx", "sub"), 1)
        arrived.append((moving_k, moving_v))
    arrived = arrived[::-1]
    key_span = jnp.concatenate([pair[0] for pair in arrived] + [own_keys], axis=0)
    value_span = jnp.concatenate([pair[1] for pair in arrived] + [own_values], axis=0)
    query_pos = first_row + jnp.arange(block_rows, dtype=jnp.int32)
    key_pos = first_row - margin_rows + jnp.arange(key_count, dtype=jnp.int32)
    lowest = jnp.maximum(doc_start_of(doc_starts[0], query_pos), query_pos - window + 1)
    grad_q, grad_k_span, grad_v_span = attend_block(
        query_heads[0], key_span, value_span, grad_out[0], query_pos, key_pos, lowest
    )

    def own_piece(distance):
        begin = (reach_blocks - distance) * block_rows
        return (grad_k_span[begin : begin + block_rows], grad_v_span[begin : begin + block_rows])

    total_k, total_v = own_piece(reach_blocks)
    for distance in range(reach_blocks - 1, -1, -1):
        moved_k, moved_v = (
            passed_along(total_k.astype(jnp.bfloat16), ("ctx", "sub"), -1).astype(total_k.dtype),
            passed_along(total_v.astype(jnp.bfloat16), ("ctx", "sub"), -1).astype(total_v.dtype),
        )
        piece_k, piece_v = own_piece(distance)
        total_k = moved_k + piece_k
        total_v = moved_v + piece_v
    grad_key = total_k.astype(jnp.bfloat16)
    grad_value = total_v.astype(jnp.bfloat16)
    contract = (((0,), (0,)), ((), ()))
    term_v = lax.dot_general(
        layer_input[0], grad_value, contract, preferred_element_type=jnp.float32
    )
    shard_v = lax.psum_scatter(term_v.astype(jnp.bfloat16), "fsdp", scatter_dimension=0, tiled=True)
    weight_v = lax.psum(shard_v, ("ctx", "sub")).astype(jnp.float32)
    token_scale = float(lax.axis_size("fsdp") * lax.axis_size(("ctx", "sub")) * block_rows) ** (
        -0.5
    )
    return (
        grad_q.astype(jnp.bfloat16)[None],
        grad_key[None],
        grad_value[None],
        weight_v * token_scale,
    )


def solution(mesh):
    placed = (
        P(("groups", "fsdp"), ("ctx", "sub"), None),
        P(("groups", "fsdp"), ("ctx", "sub"), None),
        P(("groups", "fsdp"), ("ctx", "sub"), None),
        P(("groups", "fsdp"), ("ctx", "sub"), None),
        P(("groups", "fsdp"), ("ctx", "sub"), None),
        P(("groups", "fsdp"), None),
    )
    return jax.shard_map(
        body,
        mesh=mesh,
        in_specs=placed,
        out_specs=(
            P(("groups", "fsdp"), ("ctx", "sub"), None),
            P(("groups", "fsdp"), ("ctx", "sub"), None),
            P(("groups", "fsdp"), ("ctx", "sub"), None),
            P(("groups", "fsdp"), None),
        ),
        check_vma=False,
    )
```

profile of v0, /device:TPU:0, one launch (start us, length us, event | category | flops | bytes accessed | tf_op | source)
XLA Modules:
  0.0 211.9 jit_solution(1971740638180802092)
XLA Ops:
  8.4 2.4 %collective-permute-start = (bf16[256,512]{0,1:T(8,128)(2,1)S(1)}, bf16[256,512]{0,1:T(8,128)(2,1)S(1)}, u32[]{:S(2)}, u32[]{:S(2)}) collective-permute-start(bf16[256,512]{0,1:T(8,128)(2,1)S(1)} %bitcast.186), channel_id=1, source_target_pairs={{0,1},{1,4},{4,5},{5,8},{8,9},{9,12},{12,13},{2,3},{3,6},{6,7},{7,... | collective-permute-start | bytes 786440 | tf_op jit(solution)/shard_map/ppermute | solution.py:13
  11.9 4.6 %collective-permute-start.3 = (bf16[256,512]{0,1:T(8,128)(2,1)S(1)}, bf16[256,512]{0,1:T(8,128)(2,1)S(1)}, u32[]{:S(2)}, u32[]{:S(2)}) collective-permute-start(bf16[256,512]{0,1:T(8,128)(2,1)S(1)} %bitcast.184), channel_id=1, source_target_pairs={{0,1},{1,4},{4,5},{5,8},{8,9},{9,12},{12,13},{2,3},{3,6},{6,7},{7,... | collective-permute-start | bytes 786440 | tf_op jit(solution)/shard_map/ppermute | solution.py:13
  16.5 2.2 %collective-permute-start.1 = (bf16[256,512]{0,1:T(8,128)(2,1)S(1)}, bf16[256,512]{0,1:T(8,128)(2,1)S(1)}, u32[]{:S(2)}, u32[]{:S(2)}) collective-permute-start(bf16[256,512]{0,1:T(8,128)(2,1)S(1)} %collective-permute-done), channel_id=1, source_target_pairs={{0,1},{1,4},{4,5},{5,8},{8,9},{9,12},{12,13},{2,3},{3,6},{6,7},{7,... | collective-permute-start | bytes 786440 | tf_op jit(solution)/shard_map/ppermute | solution.py:13
  18.7 4.4 %collective-permute-start.4 = (bf16[256,512]{0,1:T(8,128)(2,1)S(1)}, bf16[256,512]{0,1:T(8,128)(2,1)S(1)}, u32[]{:S(2)}, u32[]{:S(2)}) collective-permute-start(bf16[256,512]{0,1:T(8,128)(2,1)S(1)} %collective-permute-done.3), channel_id=1, source_target_pairs={{0,1},{1,4},{4,5},{5,8},{8,9},{9,12},{12,13},{2,3},{3,6},{6,7},{7,... | collective-permute-start | bytes 786440 | tf_op jit(solution)/shard_map/ppermute | solution.py:13
  23.9 3.7 %collective-permute-start.2 = (bf16[256,512]{0,1:T(8,128)(2,1)S(1)}, bf16[256,512]{0,1:T(8,128)(2,1)}, u32[]{:S(2)}, u32[]{:S(2)}) collective-permute-start(bf16[256,512]{0,1:T(8,128)(2,1)S(1)} %collective-permute-done.1), channel_id=1, source_target_pairs={{0,1},{1,4},{4,5},{5,8},{8,9},{9,12},{12,13},{2,3},{3,6},{6,7},{7,... | collective-permute-start | bytes 786440 | tf_op jit(solution)/shard_map/ppermute | solution.py:13
  27.6 3.2 %collective-permute-start.5 = (bf16[256,512]{0,1:T(8,128)(2,1)S(1)}, bf16[256,512]{0,1:T(8,128)(2,1)S(1)}, u32[]{:S(2)}, u32[]{:S(2)}) collective-permute-start(bf16[256,512]{0,1:T(8,128)(2,1)S(1)} %collective-permute-done.4), channel_id=1, source_target_pairs={{0,1},{1,4},{4,5},{5,8},{8,9},{9,12},{12,13},{2,3},{3,6},{6,7},{7,... | collective-permute-start | bytes 786440 | tf_op jit(solution)/shard_map/ppermute | solution.py:13
  30.8 2.1 copy.73
  33.9 2.1 pad_maximum_fusion
  37.1 37.4 %while.15 = (s32[]{:T(128)}, bf16[2,256,2,256]{1,3,2,0:T(8,128)(2,1)}, f32[2,1024,256]{2,1,0:T(8,128)}, f32[2,1024,256]{2,1,0:T(8,128)}, s32[2]{0:T(128)S(1)}, /...) while((s32[]{:T(128)}, ...), condition=%wide.region_5.6_spmd.clone, body=%wide.region_1.5_spmd.clone.sunk | while | flops 1353977856 | bytes 29120200 | solution.py:54
  39.9 3.5 %fusion.90 = (f32[2,256]{1,0:T(2,128)S(1)}, f32[2,256,1024]{1,2,0:T(8,128)}) fusion(pred[256,1024]{0,1:T(8,128)(4,1)S(1)} %compare_and_fusion.2, bf16[256,2,2,256]{0,3,2,1:T(8,128)(2,1)} %get-tuple-element.287, s32[]{:T(128)S(6)} %select_n.34, bf16[1024,2,256]{0,2,1:T(8,128)(2,1)} %get-tuple-element.286), kind=kOutput, calls=%fused_computation.80.clone.1 | convolution fusion | flops 271057920 | bytes 3410944 | tf_op jit(solution)/shard_map/while/body/eval_jaxpr/sub | solution.py:43
  45.0 3.9 %fusion.92 = f32[2,1024,256]{2,1,0:T(8,128)} fusion(f32[2,1024,256]{2,1,0:T(8,128)} %get-tuple-element.268, s32[]{:T(128)} %get-tuple-element.266, f32[1024,256,2]{1,0,2:T(8,128)S(1)} %fusion.89, bf16[256,2,2,256]{0,3,2,1:T(8,128)(2,1)} %get-tuple-element.287, s32[]{:T(128)S(6)} %select_n.34, f32[2,256,1024]{1,2,0:T(8,128)} %get-tuple-element.249, ...), kind=kOutput, calls=%fused_computation.14.clone.1 | convolution fusion | flops 272107008 | bytes 9703940 | tf_op jit(solution)/shard_map/while/body/eval_jaxpr/htk,thd->kd/dot_general | solution.py:50
  48.9 3.0 %fusion.93 = f32[2,1024,256]{2,1,0:T(8,128)} fusion(f32[2,1024,256]{2,1,0:T(8,128)} %get-tuple-element.269, s32[]{:T(128)} %get-tuple-element.266, bf16[256,2,2,256]{0,3,2,1:T(8,128)(2,1)} %get-tuple-element.289, s32[]{:T(128)S(6)} %select_n.34, f32[2,256,1024]{1,2,0:T(8,128)} %get-tuple-element.249, f32[2,256]{1,0:T(2,128)S(1)} %get-tuple-element.250), kind=kOutput, calls=%fused_computation.12.clone.1 | convolution fusion | flops 269484032 | bytes 3410436 | tf_op jit(solution)/shard_map/while/body/eval_jaxpr/htk,thd->kd/dot_general | solution.py:51
  51.9 3.9 %fusion.91 = bf16[2,256,2,256]{1,3,2,0:T(8,128)(2,1)} fusion(bf16[2,256,2,256]{1,3,2,0:T(8,128)(2,1)} %get-tuple-element.267, s32[]{:T(128)} %get-tuple-element.266, f32[1024,256,2]{1,0,2:T(8,128)S(1)} %fusion.89, bf16[1024,2,256]{0,2,1:T(8,128)(2,1)} %get-tuple-element.286, s32[]{:T(128)S(6)} %select_n.34, f32[2,256,1024]{1,2,0:T(8,128)} %get-tuple-element.249, ...), kind=kOutput, calls=%fused_computation.16.clone.1 | convolution fusion | flops 272107008 | bytes 9441796 | tf_op jit(solution)/shard_map/while/body/eval_jaxpr/htk,kd->thd/dot_general | solution.py:49
  58.6 3.5 %fusion.90 = (f32[2,256]{1,0:T(2,128)S(1)}, f32[2,256,1024]{1,2,0:T(8,128)}) fusion(pred[256,1024]{0,1:T(8,128)(4,1)S(1)} %compare_and_fusion.2, bf16[256,2,2,256]{0,3,2,1:T(8,128)(2,1)} %get-tuple-element.287, s32[]{:T(128)S(6)} %select_n.34, bf16[1024,2,256]{0,2,1:T(8,128)(2,1)} %get-tuple-element.286), kind=kOutput, calls=%fused_computation.80.clone.1 | convolution fusion | flops 271057920 | bytes 3410944 | tf_op jit(solution)/shard_map/while/body/eval_jaxpr/sub | solution.py:43
  63.6 4.0 %fusion.92 = f32[2,1024,256]{2,1,0:T(8,128)} fusion(f32[2,1024,256]{2,1,0:T(8,128)} %get-tuple-element.268, s32[]{:T(128)} %get-tuple-element.266, f32[1024,256,2]{1,0,2:T(8,128)S(1)} %fusion.89, bf16[256,2,2,256]{0,3,2,1:T(8,128)(2,1)} %get-tuple-element.287, s32[]{:T(128)S(6)} %select_n.34, f32[2,256,1024]{1,2,0:T(8,128)} %get-tuple-element.249, ...), kind=kOutput, calls=%fused_computation.14.clone.1 | convolution fusion | flops 272107008 | bytes 9703940 | tf_op jit(solution)/shard_map/while/body/eval_jaxpr/htk,thd->kd/dot_general | solution.py:50
  67.6 3.0 %fusion.93 = f32[2,1024,256]{2,1,0:T(8,128)} fusion(f32[2,1024,256]{2,1,0:T(8,128)} %get-tuple-element.269, s32[]{:T(128)} %get-tuple-element.266, bf16[256,2,2,256]{0,3,2,1:T(8,128)(2,1)} %get-tuple-element.289, s32[]{:T(128)S(6)} %select_n.34, f32[2,256,1024]{1,2,0:T(8,128)} %get-tuple-element.249, f32[2,256]{1,0:T(2,128)S(1)} %get-tuple-element.250), kind=kOutput, calls=%fused_computation.12.clone.1 | convolution fusion | flops 269484032 | bytes 3410436 | tf_op jit(solution)/shard_map/while/body/eval_jaxpr/htk,thd->kd/dot_general | solution.py:51
  70.7 3.9 %fusion.91 = bf16[2,256,2,256]{1,3,2,0:T(8,128)(2,1)} fusion(bf16[2,256,2,256]{1,3,2,0:T(8,128)(2,1)} %get-tuple-element.267, s32[]{:T(128)} %get-tuple-element.266, f32[1024,256,2]{1,0,2:T(8,128)S(1)} %fusion.89, bf16[1024,2,256]{0,2,1:T(8,128)(2,1)} %get-tuple-element.286, s32[]{:T(128)S(6)} %select_n.34, f32[2,256,1024]{1,2,0:T(8,128)} %get-tuple-element.249, ...), kind=kOutput, calls=%fused_computation.16.clone.1 | convolution fusion | flops 272107008 | bytes 9441796 | tf_op jit(solution)/shard_map/while/body/eval_jaxpr/htk,kd->thd/dot_general | solution.py:49
  81.1 6.3 %collective-permute-done.10 = bf16[256,512]{1,0:T(8,128)(2,1)S(1)} collective-permute-done((bf16[256,512]{1,0:T(8,128)(2,1)S(1)}, bf16[256,512]{1,0:T(8,128)(2,1)S(1)}, u32[]{:S(2)}, u32[]{:S(2)}) %collective-permute-start.10) | collective-permute-done | bytes 262176 | tf_op jit(solution)/shard_map/ppermute | solution.py:13
  88.9 6.3 %collective-permute-done.11 = bf16[256,512]{1,0:T(8,128)(2,1)S(1)} collective-permute-done((bf16[256,512]{1,0:T(8,128)(2,1)S(1)}, bf16[256,512]{1,0:T(8,128)(2,1)S(1)}, u32[]{:S(2)}, u32[]{:S(2)}) %collective-permute-start.11) | collective-permute-done | bytes 262176 | tf_op jit(solution)/shard_map/ppermute | solution.py:13
  96.7 2.4 %copy.92 = bf16[2304,512]{1,0:T(8,128)(2,1)} copy(bf16[2304,512]{0,1:T(8,128)(2,1)S(1)} %fusion.57) | data formatting | bytes 4718592
  103.2 4.9 %collective-permute-done.6 = bf16[256,512]{1,0:T(8,128)(2,1)S(1)} collective-permute-done((bf16[256,512]{1,0:T(8,128)(2,1)S(1)}, bf16[256,512]{1,0:T(8,128)(2,1)S(1)}, u32[]{:S(2)}, u32[]{:S(2)}) %collective-permute-start.6) | collective-permute-done | bytes 262176 | tf_op jit(solution)/shard_map/ppermute | solution.py:13
  110.2 28.5 %reduce-scatter.4.cloned.1.call-done = bf16[1152,512]{1,0:T(8,128)(2,1)} async-done(((bf16[2304,512]{1,0:T(8,128)(2,1)}), bf16[1152,512]{1,0:T(8,128)(2,1)}) %reduce-scatter.4.cloned.1.call-update) | async-done | bytes 1179664
  138.7 2.4 %copy.93 = bf16[1152,512]{0,1:T(8,128)(2,1)} copy(bf16[1152,512]{1,0:T(8,128)(2,1)} %reduce-scatter.4.cloned.1.call-done) | data formatting | bytes 2359296
  148.4 53.2 %all-reduce.2.cloned.1.call-done = bf16[1152,512]{0,1:T(8,128)(2,1)} async-done(((bf16[1152,512]{0,1:T(8,128)(2,1)}), bf16[1152,512]{0,1:T(8,128)(2,1)}) %all-reduce.2.cloned.1.call-update) | async-done | bytes 1179664 | tf_op jit(solution)/shard_map/psum | solution.py:106
  (73 shorter events, 36.4 us)
Async XLA Ops:
  7.2 88.7 %copy-start = (bf16[1,256,2304]{2,1,0:T(8,128)(2,1)S(1)}, bf16[1,256,2304]{2,1,0:T(8,128)(2,1)}, u32[]{:S(2)}) copy-start(bf16[1,256,2304]{2,1,0:T(8,128)(2,1)} %param.8) | copy-start | bytes 3538948
  7.2 25.7 %copy-start.5 = (bf16[1,256,1024]{2,1,0:T(8,128)(2,1)S(1)}, bf16[1,256,1024]{2,1,0:T(8,128)(2,1)}, u32[]{:S(2)}) copy-start(bf16[1,256,1024]{2,1,0:T(8,128)(2,1)} %param.9) | copy-start | bytes 1572868
  7.2 131.5 %reduce-scatter.4.cloned.1.call-start = ((), (), s32[]{:S(2)}) async-start(), calls=%async_computation.2 | async-start | bytes 3538944
  8.4 8.1 %collective-permute-start = (bf16[256,512]{0,1:T(8,128)(2,1)S(1)}, bf16[256,512]{0,1:T(8,128)(2,1)S(1)}, u32[]{:S(2)}, u32[]{:S(2)}) collective-permute-start(bf16[256,512]{0,1:T(8,128)(2,1)S(1)} %bitcast.186), channel_id=1, source_target_pairs={{0,1},{1,4},{4,5},{5,8},{8,9},{9,12},{12,13},{2,3},{3,6},{6,7},{7,... | collective-permute-start | bytes 786440 | tf_op jit(solution)/shard_map/ppermute | solution.py:13
  11.9 6.8 %collective-permute-start.3 = (bf16[256,512]{0,1:T(8,128)(2,1)S(1)}, bf16[256,512]{0,1:T(8,128)(2,1)S(1)}, u32[]{:S(2)}, u32[]{:S(2)}) collective-permute-start(bf16[256,512]{0,1:T(8,128)(2,1)S(1)} %bitcast.184), channel_id=1, source_target_pairs={{0,1},{1,4},{4,5},{5,8},{8,9},{9,12},{12,13},{2,3},{3,6},{6,7},{7,... | collective-permute-start | bytes 786440 | tf_op jit(solution)/shard_map/ppermute | solution.py:13
  16.5 7.4 %collective-permute-start.1 = (bf16[256,512]{0,1:T(8,128)(2,1)S(1)}, bf16[256,512]{0,1:T(8,128)(2,1)S(1)}, u32[]{:S(2)}, u32[]{:S(2)}) collective-permute-start(bf16[256,512]{0,1:T(8,128)(2,1)S(1)} %collective-permute-done), channel_id=1, source_target_pairs={{0,1},{1,4},{4,5},{5,8},{8,9},{9,12},{12,13},{2,3},{3,6},{6,7},{7,... | collective-permute-start | bytes 786440 | tf_op jit(solution)/shard_map/ppermute | solution.py:13
  18.7 8.9 %collective-permute-start.4 = (bf16[256,512]{0,1:T(8,128)(2,1)S(1)}, bf16[256,512]{0,1:T(8,128)(2,1)S(1)}, u32[]{:S(2)}, u32[]{:S(2)}) collective-permute-start(bf16[256,512]{0,1:T(8,128)(2,1)S(1)} %collective-permute-done.3), channel_id=1, source_target_pairs={{0,1},{1,4},{4,5},{5,8},{8,9},{9,12},{12,13},{2,3},{3,6},{6,7},{7,... | collective-permute-start | bytes 786440 | tf_op jit(solution)/shard_map/ppermute | solution.py:13
  23.9 10.0 %collective-permute-start.2 = (bf16[256,512]{0,1:T(8,128)(2,1)S(1)}, bf16[256,512]{0,1:T(8,128)(2,1)}, u32[]{:S(2)}, u32[]{:S(2)}) collective-permute-start(bf16[256,512]{0,1:T(8,128)(2,1)S(1)} %collective-permute-done.1), channel_id=1, source_target_pairs={{0,1},{1,4},{4,5},{5,8},{8,9},{9,12},{12,13},{2,3},{3,6},{6,7},{7,... | collective-permute-start | bytes 786440 | tf_op jit(solution)/shard_map/ppermute | solution.py:13
  27.6 8.4 %collective-permute-start.5 = (bf16[256,512]{0,1:T(8,128)(2,1)S(1)}, bf16[256,512]{0,1:T(8,128)(2,1)S(1)}, u32[]{:S(2)}, u32[]{:S(2)}) collective-permute-start(bf16[256,512]{0,1:T(8,128)(2,1)S(1)} %collective-permute-done.4), channel_id=1, source_target_pairs={{0,1},{1,4},{4,5},{5,8},{8,9},{9,12},{12,13},{2,3},{3,6},{6,7},{7,... | collective-permute-start | bytes 786440 | tf_op jit(solution)/shard_map/ppermute | solution.py:13
  75.6 4.0 %collective-permute-start.9 = (bf16[256,512]{1,0:T(8,128)(2,1)S(1)}, bf16[256,512]{1,0:T(8,128)(2,1)S(1)}, u32[]{:S(2)}, u32[]{:S(2)}) collective-permute-start(bf16[256,512]{1,0:T(8,128)(2,1)S(1)} %bitcast.189), channel_id=1, source_target_pairs={{1,0},{4,1},{5,4},{8,5},{9,8},{12,9},{13,12},{3,2},{6,3},{7,6},{10... | collective-permute-start | bytes 786440 | tf_op jit(solution)/shard_map/ppermute | solution.py:13
  79.7 7.7 %collective-permute-start.10 = (bf16[256,512]{1,0:T(8,128)(2,1)S(1)}, bf16[256,512]{1,0:T(8,128)(2,1)S(1)}, u32[]{:S(2)}, u32[]{:S(2)}) collective-permute-start(bf16[256,512]{1,0:T(8,128)(2,1)S(1)} %add_convert_fusion.2), channel_id=1, source_target_pairs={{1,0},{4,1},{5,4},{8,5},{9,8},{12,9},{13,12},{3,2},{6,3},{7,6},{10... | collective-permute-start | bytes 786440 | tf_op jit(solution)/shard_map/ppermute | solution.py:13
  87.5 7.7 %collective-permute-start.11 = (bf16[256,512]{1,0:T(8,128)(2,1)S(1)}, bf16[256,512]{1,0:T(8,128)(2,1)S(1)}, u32[]{:S(2)}, u32[]{:S(2)}) collective-permute-start(bf16[256,512]{1,0:T(8,128)(2,1)S(1)} %add_convert_fusion.1), channel_id=1, source_target_pairs={{1,0},{4,1},{5,4},{8,5},{9,8},{12,9},{13,12},{3,2},{6,3},{7,6},{10... | collective-permute-start | bytes 786440 | tf_op jit(solution)/shard_map/ppermute | solution.py:13
  88.9 6.3 %copy-start.1 = (f32[2,32,8,256]{3,2,0,1:T(8,128)}, f32[2,32,8,256]{3,2,0,1:T(8,128)S(1)}, u32[]{:S(2)}) copy-start(f32[2,32,8,256]{3,2,0,1:T(8,128)S(1)} %copy.105) | copy-start | bytes 1572868
  95.2 0.7 copy-start.3
  99.2 102.4 %all-reduce.2.cloned.1.call-start = ((), (), s32[]{:S(2)}) async-start(), calls=%async_computation.1 | async-start | bytes 2359296 | tf_op jit(solution)/shard_map/psum | solution.py:106
  100.4 7.7 %collective-permute-start.6 = (bf16[256,512]{1,0:T(8,128)(2,1)S(1)}, bf16[256,512]{1,0:T(8,128)(2,1)S(1)}, u32[]{:S(2)}, u32[]{:S(2)}) collective-permute-start(bf16[256,512]{1,0:T(8,128)(2,1)S(1)} %bitcast.190), channel_id=1, source_target_pairs={{1,0},{4,1},{5,4},{8,5},{9,8},{12,9},{13,12},{3,2},{6,3},{7,6},{10... | collective-permute-start | bytes 786440 | tf_op jit(solution)/shard_map/ppermute | solution.py:13
  108.8 32.3 %collective-permute-start.7 = (bf16[256,512]{1,0:T(8,128)(2,1)}, bf16[256,512]{1,0:T(8,128)(2,1)}, u32[]{:S(2)}, u32[]{:S(2)}) collective-permute-start(bf16[256,512]{1,0:T(8,128)(2,1)} %add_convert_fusion.5), channel_id=1, source_target_pairs={{1,0},{4,1},{5,4},{8,5},{9,8},{12,9},{13,12},{3,2},{6,3},{7,6},{10... | collective-permute-start | bytes 786440 | tf_op jit(solution)/shard_map/ppermute | solution.py:13
  141.1 3.2 %copy-start.6 = (bf16[2,256,2,256]{1,3,2,0:T(8,128)(2,1)S(1)}, bf16[2,256,2,256]{1,3,2,0:T(8,128)(2,1)}, u32[]{:S(2)}) copy-start(bf16[2,256,2,256]{1,3,2,0:T(8,128)(2,1)} %get-tuple-element.58) | copy-start | bytes 1572868
  141.1 4.2 %copy-start.2 = (f32[2,32,8,256]{3,2,0,1:T(8,128)S(1)}, f32[2,32,8,256]{3,2,0,1:T(8,128)}, u32[]{:S(2)}) copy-start(f32[2,32,8,256]{3,2,0,1:T(8,128)} %copy-done.1) | copy-start | bytes 1572868
  141.1 4.2 %copy-start.4 = (bf16[256,512]{1,0:T(8,128)(2,1)S(1)}, bf16[256,512]{1,0:T(8,128)(2,1)}, u32[]{:S(2)}) copy-start(bf16[256,512]{1,0:T(8,128)(2,1)} %copy-done.3) | copy-start | bytes 786436
  142.9 3.8 %collective-permute-start.8 = (bf16[256,512]{1,0:T(8,128)(2,1)}, bf16[256,512]{1,0:T(8,128)(2,1)}, u32[]{:S(2)}, u32[]{:S(2)}) collective-permute-start(bf16[256,512]{1,0:T(8,128)(2,1)} %add_convert_fusion.4), channel_id=1, source_target_pairs={{1,0},{4,1},{5,4},{8,5},{9,8},{12,9},{13,12},{3,2},{6,3},{7,6},{10... | collective-permute-start | bytes 786440 | tf_op jit(solution)/shard_map/ppermute | solution.py:13
Sparse Core Ops, SparseCore 0:
  99.3 39.3 reduce-scatter.3
  141.7 59.8 all-reduce.1
where the time goes:
time: 213 us; the launch traced here: 212 us
  waiting for transfers between devices  101 us (47%)
  matrix products  32.6 us (15%)
  starting transfers between devices  28.2 us (13%)
  local copies, waits for them, and re-layouts  20.5 us (10%)
  between operations  14.4 us (7%)
  other arithmetic  11.2 us (5%)
  loops' own time  3.92 us (2%)
    psum x1, waiting for transfers between devices, body(): weight_v = lax.psum(shard_v, ('ctx', 'sub')).astype(jnp.float32)  53.2 us
    unnamed x3, waiting for transfers between devices  28.5 us
    ppermute x12, starting transfers between devices, passed_along(): lax.ppermute(value, axis, [(source, source + steps) for source in range(f...  28.2 us
    ppermute x12, waiting for transfers between devices, passed_along(): lax.ppermute(value, axis, [(source, source + steps) for source in range(f...  19.3 us
    unnamed x25, local copies, waits for them, and re-layouts  17.9 us
    dot_general x2, matrix products, one_group(): jnp.einsum('htk,thd->kd', grad_scores, query_g, preferred_element_type=jn...  7.91 us
    dot_general x2, matrix products, one_group(): jnp.einsum('htk,kd->thd', grad_scores, key_g, preferred_element_type=jnp....  7.74 us
    sub x2, matrix products, one_group(): raised = jnp.where(allowed[None], jnp.exp(scores - largest), 0.0)  6.91 us
  transfers between devices with their start and end apart: 14, of which 7 were waited for; matrix products, arithmetic and copies ran while one was open for 9% of the time, Pallas kernels for 0%

commit v1 on v0

--- a/solution.py
+++ b/solution.py
@@ -2,6 +2,7 @@
 import jax.numpy as jnp
 from jax import lax
 from jax.sharding import PartitionSpec as P
+from jax.lax import psum
 
 HEAD_DIM = 256
 SPAN = 768
@@ -103,7 +104,7 @@
         layer_input[0], grad_value, contract, preferred_element_type=jnp.float32
     )
     shard_v = lax.psum_scatter(term_v.astype(jnp.bfloat16), "fsdp", scatter_dimension=0, tiled=True)
-    weight_v = lax.psum(shard_v, ("ctx", "sub")).astype(jnp.float32)
+    weight_v = psum(psum(shard_v, "sub"), "ctx").astype(jnp.float32)
     token_scale = float(lax.axis_size("fsdp") * lax.axis_size(("ctx", "sub")) * block_rows) ** (
         -0.5
     )

time: 213 us -> 235 us (1.10)
  waiting for transfers between devices: 101 us -> 123 us
    unnamed x3 -> x4, waiting for transfers between devices: 28.5 us -> 39.5 us
    psum x1 -> x2, waiting for transfers between devices: 53.2 us -> 63.3 us  [body(): weight_v = psum(psum(shard_v, 'sub'), 'ctx').astype(jnp.float32)]
    unnamed x25 -> x27, local copies, waits for them, and re-layouts: 17.9 us -> 18.6 us
  transfers between devices with their start and end apart: 14 -> 15, of which waited for: 7 -> 8; matrix products, arithmetic and copies ran while one was open for 9% -> 7% of each run, Pallas kernels for 0% -> 0%
where the time goes in v1:
time: 235 us; the launch traced here: 234 us
  waiting for transfers between devices  123 us (52%)
  matrix products  32.6 us (14%)
  starting transfers between devices  28.3 us (12%)
  local copies, waits for them, and re-layouts  21.2 us (9%)
  between operations  14.1 us (6%)
  other arithmetic  10.4 us (4%)
  loops' own time  3.92 us (2%)
    psum x2, waiting for transfers between devices, body(): weight_v = psum(psum(shard_v, 'sub'), 'ctx').astype(jnp.float32)  63.3 us
    unnamed x4, waiting for transfers between devices  39.5 us
    ppermute x12, starting transfers between devices, passed_along(): lax.ppermute(value, axis, [(source, source + steps) for source in range(f...  28.2 us
    ppermute x12, waiting for transfers between devices, passed_along(): lax.ppermute(value, axis, [(source, source + steps) for source in range(f...  20.5 us
    unnamed x27, local copies, waits for them, and re-layouts  18.6 us
    dot_general x2, matrix products, one_group(): jnp.einsum('htk,thd->kd', grad_scores, query_g, preferred_element_type=jn...  7.9 us
    dot_general x2, matrix products, one_group(): jnp.einsum('htk,kd->thd', grad_scores, key_g, preferred_element_type=jnp....  7.74 us
    sub x2, matrix products, one_group(): raised = jnp.where(allowed[None], jnp.exp(scores - largest), 0.0)  6.94 us
  transfers between devices with their start and end apart: 15, of which 8 were waited for; matrix products, arithmetic and copies ran while one was open for 7% of the time, Pallas kernels for 0%

profile of v1, /device:TPU:0, one launch (start us, length us, event | category | flops | bytes accessed | tf_op | source)
XLA Modules:
  0.0 233.8 jit_solution(2710563306042020541)
XLA Ops:
  8.4 2.4 %collective-permute-start = (bf16[256,512]{0,1:T(8,128)(2,1)S(1)}, bf16[256,512]{0,1:T(8,128)(2,1)S(1)}, u32[]{:S(2)}, u32[]{:S(2)}) collective-permute-start(bf16[256,512]{0,1:T(8,128)(2,1)S(1)} %bitcast.186), channel_id=1, source_target_pairs={{0,1},{1,4},{4,5},{5,8},{8,9},{9,12},{12,13},{2,3},{3,6},{6,7},{7,... | collective-permute-start | bytes 786440 | tf_op jit(solution)/shard_map/ppermute | solution.py:14
  11.9 4.6 %collective-permute-start.3 = (bf16[256,512]{0,1:T(8,128)(2,1)S(1)}, bf16[256,512]{0,1:T(8,128)(2,1)S(1)}, u32[]{:S(2)}, u32[]{:S(2)}) collective-permute-start(bf16[256,512]{0,1:T(8,128)(2,1)S(1)} %bitcast.184), channel_id=1, source_target_pairs={{0,1},{1,4},{4,5},{5,8},{8,9},{9,12},{12,13},{2,3},{3,6},{6,7},{7,... | collective-permute-start | bytes 786440 | tf_op jit(solution)/shard_map/ppermute | solution.py:14
  16.5 2.2 collective-permute-start.1
  18.7 4.4 %collective-permute-start.4 = (bf16[256,512]{0,1:T(8,128)(2,1)S(1)}, bf16[256,512]{0,1:T(8,128)(2,1)S(1)}, u32[]{:S(2)}, u32[]{:S(2)}) collective-permute-start(bf16[256,512]{0,1:T(8,128)(2,1)S(1)} %collective-permute-done.3), channel_id=1, source_target_pairs={{0,1},{1,4},{4,5},{5,8},{8,9},{9,12},{12,13},{2,3},{3,6},{6,7},{7,... | collective-permute-start | bytes 786440 | tf_op jit(solution)/shard_map/ppermute | solution.py:14
  23.9 3.7 %collective-permute-start.2 = (bf16[256,512]{0,1:T(8,128)(2,1)S(1)}, bf16[256,512]{0,1:T(8,128)(2,1)}, u32[]{:S(2)}, u32[]{:S(2)}) collective-permute-start(bf16[256,512]{0,1:T(8,128)(2,1)S(1)} %collective-permute-done.1), channel_id=1, source_target_pairs={{0,1},{1,4},{4,5},{5,8},{8,9},{9,12},{12,13},{2,3},{3,6},{6,7},{7,... | collective-permute-start | bytes 786440 | tf_op jit(solution)/shard_map/ppermute | solution.py:14
  27.6 3.2 %collective-permute-start.5 = (bf16[256,512]{0,1:T(8,128)(2,1)S(1)}, bf16[256,512]{0,1:T(8,128)(2,1)S(1)}, u32[]{:S(2)}, u32[]{:S(2)}) collective-permute-start(bf16[256,512]{0,1:T(8,128)(2,1)S(1)} %collective-permute-done.4), channel_id=1, source_target_pairs={{0,1},{1,4},{4,5},{5,8},{8,9},{9,12},{12,13},{2,3},{3,6},{6,7},{7,... | collective-permute-start | bytes 786440 | tf_op jit(solution)/shard_map/ppermute | solution.py:14
  33.9 2.1 pad_maximum_fusion
  37.1 37.4 %while.15 = (s32[]{:T(128)}, bf16[2,256,2,256]{1,3,2,0:T(8,128)(2,1)}, f32[2,1024,256]{2,1,0:T(8,128)}, f32[2,1024,256]{2,1,0:T(8,128)}, s32[2]{0:T(128)S(1)}, /...) while((s32[]{:T(128)}, ...), condition=%wide.region_5.6_spmd.clone, body=%wide.region_1.5_spmd.clone.sunk | while | flops 1353977856 | bytes 29120200 | solution.py:55
  39.9 3.5 %fusion.90 = (f32[2,256]{1,0:T(2,128)S(1)}, f32[2,256,1024]{1,2,0:T(8,128)}) fusion(pred[256,1024]{0,1:T(8,128)(4,1)S(1)} %compare_and_fusion.2, bf16[256,2,2,256]{0,3,2,1:T(8,128)(2,1)} %get-tuple-element.287, s32[]{:T(128)S(6)} %select_n.34, bf16[1024,2,256]{0,2,1:T(8,128)(2,1)} %get-tuple-element.286), kind=kOutput, calls=%fused_computation.80.clone.1 | convolution fusion | flops 271057920 | bytes 3410944 | tf_op jit(solution)/shard_map/while/body/eval_jaxpr/sub | solution.py:44
  45.0 3.9 %fusion.92 = f32[2,1024,256]{2,1,0:T(8,128)} fusion(f32[2,1024,256]{2,1,0:T(8,128)} %get-tuple-element.268, s32[]{:T(128)} %get-tuple-element.266, f32[1024,256,2]{1,0,2:T(8,128)S(1)} %fusion.89, bf16[256,2,2,256]{0,3,2,1:T(8,128)(2,1)} %get-tuple-element.287, s32[]{:T(128)S(6)} %select_n.34, f32[2,256,1024]{1,2,0:T(8,128)} %get-tuple-element.249, ...), kind=kOutput, calls=%fused_computation.14.clone.1 | convolution fusion | flops 272107008 | bytes 9703940 | tf_op jit(solution)/shard_map/while/body/eval_jaxpr/htk,thd->kd/dot_general | solution.py:51
  48.9 3.0 %fusion.93 = f32[2,1024,256]{2,1,0:T(8,128)} fusion(f32[2,1024,256]{2,1,0:T(8,128)} %get-tuple-element.269, s32[]{:T(128)} %get-tuple-element.266, bf16[256,2,2,256]{0,3,2,1:T(8,128)(2,1)} %get-tuple-element.289, s32[]{:T(128)S(6)} %select_n.34, f32[2,256,1024]{1,2,0:T(8,128)} %get-tuple-element.249, f32[2,256]{1,0:T(2,128)S(1)} %get-tuple-element.250), kind=kOutput, calls=%fused_computation.12.clone.1 | convolution fusion | flops 269484032 | bytes 3410436 | tf_op jit(solution)/shard_map/while/body/eval_jaxpr/htk,thd->kd/dot_general | solution.py:52
  51.9 3.9 %fusion.91 = bf16[2,256,2,256]{1,3,2,0:T(8,128)(2,1)} fusion(bf16[2,256,2,256]{1,3,2,0:T(8,128)(2,1)} %get-tuple-element.267, s32[]{:T(128)} %get-tuple-element.266, f32[1024,256,2]{1,0,2:T(8,128)S(1)} %fusion.89, bf16[1024,2,256]{0,2,1:T(8,128)(2,1)} %get-tuple-element.286, s32[]{:T(128)S(6)} %select_n.34, f32[2,256,1024]{1,2,0:T(8,128)} %get-tuple-element.249, ...), kind=kOutput, calls=%fused_computation.16.clone.1 | convolution fusion | flops 272107008 | bytes 9441796 | tf_op jit(solution)/shard_map/while/body/eval_jaxpr/htk,kd->thd/dot_general | solution.py:50
  58.6 3.5 %fusion.90 = (f32[2,256]{1,0:T(2,128)S(1)}, f32[2,256,1024]{1,2,0:T(8,128)}) fusion(pred[256,1024]{0,1:T(8,128)(4,1)S(1)} %compare_and_fusion.2, bf16[256,2,2,256]{0,3,2,1:T(8,128)(2,1)} %get-tuple-element.287, s32[]{:T(128)S(6)} %select_n.34, bf16[1024,2,256]{0,2,1:T(8,128)(2,1)} %get-tuple-element.286), kind=kOutput, calls=%fused_computation.80.clone.1 | convolution fusion | flops 271057920 | bytes 3410944 | tf_op jit(solution)/shard_map/while/body/eval_jaxpr/sub | solution.py:44
  63.7 4.0 %fusion.92 = f32[2,1024,256]{2,1,0:T(8,128)} fusion(f32[2,1024,256]{2,1,0:T(8,128)} %get-tuple-element.268, s32[]{:T(128)} %get-tuple-element.266, f32[1024,256,2]{1,0,2:T(8,128)S(1)} %fusion.89, bf16[256,2,2,256]{0,3,2,1:T(8,128)(2,1)} %get-tuple-element.287, s32[]{:T(128)S(6)} %select_n.34, f32[2,256,1024]{1,2,0:T(8,128)} %get-tuple-element.249, ...), kind=kOutput, calls=%fused_computation.14.clone.1 | convolution fusion | flops 272107008 | bytes 9703940 | tf_op jit(solution)/shard_map/while/body/eval_jaxpr/htk,thd->kd/dot_general | solution.py:51
  67.6 3.0 %fusion.93 = f32[2,1024,256]{2,1,0:T(8,128)} fusion(f32[2,1024,256]{2,1,0:T(8,128)} %get-tuple-element.269, s32[]{:T(128)} %get-tuple-element.266, bf16[256,2,2,256]{0,3,2,1:T(8,128)(2,1)} %get-tuple-element.289, s32[]{:T(128)S(6)} %select_n.34, f32[2,256,1024]{1,2,0:T(8,128)} %get-tuple-element.249, f32[2,256]{1,0:T(2,128)S(1)} %get-tuple-element.250), kind=kOutput, calls=%fused_computation.12.clone.1 | convolution fusion | flops 269484032 | bytes 3410436 | tf_op jit(solution)/shard_map/while/body/eval_jaxpr/htk,thd->kd/dot_general | solution.py:52
  70.7 3.9 %fusion.91 = bf16[2,256,2,256]{1,3,2,0:T(8,128)(2,1)} fusion(bf16[2,256,2,256]{1,3,2,0:T(8,128)(2,1)} %get-tuple-element.267, s32[]{:T(128)} %get-tuple-element.266, f32[1024,256,2]{1,0,2:T(8,128)S(1)} %fusion.89, bf16[1024,2,256]{0,2,1:T(8,128)(2,1)} %get-tuple-element.286, s32[]{:T(128)S(6)} %select_n.34, f32[2,256,1024]{1,2,0:T(8,128)} %get-tuple-element.249, ...), kind=kOutput, calls=%fused_computation.16.clone.1 | convolution fusion | flops 272107008 | bytes 9441796 | tf_op jit(solution)/shard_map/while/body/eval_jaxpr/htk,kd->thd/dot_general | solution.py:50
  81.1 6.3 %collective-permute-done.10 = bf16[256,512]{1,0:T(8,128)(2,1)S(1)} collective-permute-done((bf16[256,512]{1,0:T(8,128)(2,1)S(1)}, bf16[256,512]{1,0:T(8,128)(2,1)S(1)}, u32[]{:S(2)}, u32[]{:S(2)}) %collective-permute-start.10) | collective-permute-done | bytes 262176 | tf_op jit(solution)/shard_map/ppermute | solution.py:14
  88.9 6.3 %collective-permute-done.11 = bf16[256,512]{1,0:T(8,128)(2,1)S(1)} collective-permute-done((bf16[256,512]{1,0:T(8,128)(2,1)S(1)}, bf16[256,512]{1,0:T(8,128)(2,1)S(1)}, u32[]{:S(2)}, u32[]{:S(2)}) %collective-permute-start.11) | collective-permute-done | bytes 262176 | tf_op jit(solution)/shard_map/ppermute | solution.py:14
  96.7 2.4 %copy.92 = bf16[2304,512]{1,0:T(8,128)(2,1)} copy(bf16[2304,512]{0,1:T(8,128)(2,1)S(1)} %fusion.57) | data formatting | bytes 4718592
  99.3 39.4 %reduce-scatter.4.cloned.1.call-done = bf16[1152,512]{1,0:T(8,128)(2,1)} async-done(((bf16[2304,512]{1,0:T(8,128)(2,1)}), bf16[1152,512]{1,0:T(8,128)(2,1)}) %reduce-scatter.4.cloned.1.call-update) | async-done | bytes 1179664
  138.7 2.4 %copy.93 = bf16[1152,512]{0,1:T(8,128)(2,1)} copy(bf16[1152,512]{1,0:T(8,128)(2,1)} %reduce-scatter.4.cloned.1.call-done) | data formatting | bytes 2359296
  145.1 16.5 %all-reduce.3.cloned.1.call-done = bf16[1152,512]{0,1:T(8,128)(2,1)} async-done(((bf16[1152,512]{0,1:T(8,128)(2,1)}), bf16[1152,512]{0,1:T(8,128)(2,1)}) %all-reduce.3.cloned.1.call-update) | async-done | bytes 1179664 | tf_op jit(solution)/shard_map/psum | solution.py:107
  170.8 4.6 %collective-permute-done.8 = bf16[256,512]{1,0:T(8,128)(2,1)} collective-permute-done((bf16[256,512]{1,0:T(8,128)(2,1)}, bf16[256,512]{1,0:T(8,128)(2,1)}, u32[]{:S(2)}, u32[]{:S(2)}) %collective-permute-start.8) | collective-permute-done | bytes 262176 | tf_op jit(solution)/shard_map/ppermute | solution.py:14
  177.1 46.8 %all-reduce.5.cloned.1.call-done = bf16[1152,512]{0,1:T(8,128)(2,1)} async-done(((bf16[1152,512]{0,1:T(8,128)(2,1)}), bf16[1152,512]{0,1:T(8,128)(2,1)}) %all-reduce.5.cloned.1.call-update) | async-done | bytes 1179664 | tf_op jit(solution)/shard_map/psum | solution.py:107
  (78 shorter events, 39.9 us)
Async XLA Ops:
  7.2 88.7 %copy-start = (bf16[1,256,2304]{2,1,0:T(8,128)(2,1)S(1)}, bf16[1,256,2304]{2,1,0:T(8,128)(2,1)}, u32[]{:S(2)}) copy-start(bf16[1,256,2304]{2,1,0:T(8,128)(2,1)} %param.8) | copy-start | bytes 3538948
  7.2 25.7 %copy-start.5 = (bf16[1,256,1024]{2,1,0:T(8,128)(2,1)S(1)}, bf16[1,256,1024]{2,1,0:T(8,128)(2,1)}, u32[]{:S(2)}) copy-start(bf16[1,256,1024]{2,1,0:T(8,128)(2,1)} %param.9) | copy-start | bytes 1572868
  7.2 131.5 %reduce-scatter.4.cloned.1.call-start = ((), (), s32[]{:S(2)}) async-start(), calls=%async_computation.3 | async-start | bytes 3538944
  8.4 8.1 %collective-permute-start = (bf16[256,512]{0,1:T(8,128)(2,1)S(1)}, bf16[256,512]{0,1:T(8,128)(2,1)S(1)}, u32[]{:S(2)}, u32[]{:S(2)}) collective-permute-start(bf16[256,512]{0,1:T(8,128)(2,1)S(1)} %bitcast.186), channel_id=1, source_target_pairs={{0,1},{1,4},{4,5},{5,8},{8,9},{9,12},{12,13},{2,3},{3,6},{6,7},{7,... | collective-permute-start | bytes 786440 | tf_op jit(solution)/shard_map/ppermute | solution.py:14
  11.9 6.8 %collective-permute-start.3 = (bf16[256,512]{0,1:T(8,128)(2,1)S(1)}, bf16[256,512]{0,1:T(8,128)(2,1)S(1)}, u32[]{:S(2)}, u32[]{:S(2)}) collective-permute-start(bf16[256,512]{0,1:T(8,128)(2,1)S(1)} %bitcast.184), channel_id=1, source_target_pairs={{0,1},{1,4},{4,5},{5,8},{8,9},{9,12},{12,13},{2,3},{3,6},{6,7},{7,... | collective-permute-start | bytes 786440 | tf_op jit(solution)/shard_map/ppermute | solution.py:14
  16.5 7.4 %collective-permute-start.1 = (bf16[256,512]{0,1:T(8,128)(2,1)S(1)}, bf16[256,512]{0,1:T(8,128)(2,1)S(1)}, u32[]{:S(2)}, u32[]{:S(2)}) collective-permute-start(bf16[256,512]{0,1:T(8,128)(2,1)S(1)} %collective-permute-done), channel_id=1, source_target_pairs={{0,1},{1,4},{4,5},{5,8},{8,9},{9,12},{12,13},{2,3},{3,6},{6,7},{7,... | collective-permute-start | bytes 786440 | tf_op jit(solution)/shard_map/ppermute | solution.py:14
  18.7 8.9 %collective-permute-start.4 = (bf16[256,512]{0,1:T(8,128)(2,1)S(1)}, bf16[256,512]{0,1:T(8,128)(2,1)S(1)}, u32[]{:S(2)}, u32[]{:S(2)}) collective-permute-start(bf16[256,512]{0,1:T(8,128)(2,1)S(1)} %collective-permute-done.3), channel_id=1, source_target_pairs={{0,1},{1,4},{4,5},{5,8},{8,9},{9,12},{12,13},{2,3},{3,6},{6,7},{7,... | collective-permute-start | bytes 786440 | tf_op jit(solution)/shard_map/ppermute | solution.py:14
  23.9 10.0 %collective-permute-start.2 = (bf16[256,512]{0,1:T(8,128)(2,1)S(1)}, bf16[256,512]{0,1:T(8,128)(2,1)}, u32[]{:S(2)}, u32[]{:S(2)}) collective-permute-start(bf16[256,512]{0,1:T(8,128)(2,1)S(1)} %collective-permute-done.1), channel_id=1, source_target_pairs={{0,1},{1,4},{4,5},{5,8},{8,9},{9,12},{12,13},{2,3},{3,6},{6,7},{7,... | collective-permute-start | bytes 786440 | tf_op jit(solution)/shard_map/ppermute | solution.py:14
  27.6 8.4 %collective-permute-start.5 = (bf16[256,512]{0,1:T(8,128)(2,1)S(1)}, bf16[256,512]{0,1:T(8,128)(2,1)S(1)}, u32[]{:S(2)}, u32[]{:S(2)}) collective-permute-start(bf16[256,512]{0,1:T(8,128)(2,1)S(1)} %collective-permute-done.4), channel_id=1, source_target_pairs={{0,1},{1,4},{4,5},{5,8},{8,9},{9,12},{12,13},{2,3},{3,6},{6,7},{7,... | collective-permute-start | bytes 786440 | tf_op jit(solution)/shard_map/ppermute | solution.py:14
  75.6 4.0 %collective-permute-start.9 = (bf16[256,512]{1,0:T(8,128)(2,1)S(1)}, bf16[256,512]{1,0:T(8,128)(2,1)S(1)}, u32[]{:S(2)}, u32[]{:S(2)}) collective-permute-start(bf16[256,512]{1,0:T(8,128)(2,1)S(1)} %bitcast.190), channel_id=1, source_target_pairs={{1,0},{4,1},{5,4},{8,5},{9,8},{12,9},{13,12},{3,2},{6,3},{7,6},{10... | collective-permute-start | bytes 786440 | tf_op jit(solution)/shard_map/ppermute | solution.py:14
  79.7 7.7 %collective-permute-start.10 = (bf16[256,512]{1,0:T(8,128)(2,1)S(1)}, bf16[256,512]{1,0:T(8,128)(2,1)S(1)}, u32[]{:S(2)}, u32[]{:S(2)}) collective-permute-start(bf16[256,512]{1,0:T(8,128)(2,1)S(1)} %add_convert_fusion.2), channel_id=1, source_target_pairs={{1,0},{4,1},{5,4},{8,5},{9,8},{12,9},{13,12},{3,2},{6,3},{7,6},{10... | collective-permute-start | bytes 786440 | tf_op jit(solution)/shard_map/ppermute | solution.py:14
  87.5 7.7 %collective-permute-start.11 = (bf16[256,512]{1,0:T(8,128)(2,1)S(1)}, bf16[256,512]{1,0:T(8,128)(2,1)S(1)}, u32[]{:S(2)}, u32[]{:S(2)}) collective-permute-start(bf16[256,512]{1,0:T(8,128)(2,1)S(1)} %add_convert_fusion.1), channel_id=1, source_target_pairs={{1,0},{4,1},{5,4},{8,5},{9,8},{12,9},{13,12},{3,2},{6,3},{7,6},{10... | collective-permute-start | bytes 786440 | tf_op jit(solution)/shard_map/ppermute | solution.py:14
  88.9 6.3 %copy-start.1 = (f32[2,32,8,256]{3,2,0,1:T(8,128)}, f32[2,32,8,256]{3,2,0,1:T(8,128)S(1)}, u32[]{:S(2)}) copy-start(f32[2,32,8,256]{3,2,0,1:T(8,128)S(1)} %copy.105) | copy-start | bytes 1572868
  95.2 0.7 copy-start.3
  99.2 62.4 %all-reduce.3.cloned.1.call-start = ((), (), s32[]{:S(2)}) async-start(), calls=%async_computation.1 | async-start | bytes 2359296 | tf_op jit(solution)/shard_map/psum | solution.py:107
  141.1 82.8 %all-reduce.5.cloned.1.call-start = ((), (), s32[]{:S(2)}) async-start(), calls=%async_computation.2 | async-start | bytes 2359296 | tf_op jit(solution)/shard_map/psum | solution.py:107
  142.3 19.4 %collective-permute-start.6 = (bf16[256,512]{1,0:T(8,128)(2,1)S(1)}, bf16[256,512]{1,0:T(8,128)(2,1)S(1)}, u32[]{:S(2)}, u32[]{:S(2)}) collective-permute-start(bf16[256,512]{1,0:T(8,128)(2,1)S(1)} %bitcast.189), channel_id=1, source_target_pairs={{1,0},{4,1},{5,4},{8,5},{9,8},{12,9},{13,12},{3,2},{6,3},{7,6},{10... | collective-permute-start | bytes 786440 | tf_op jit(solution)/shard_map/ppermute | solution.py:14
  161.6 0.7 copy-start.7
  162.3 6.6 %copy-start.6 = (bf16[2,256,2,256]{1,3,2,0:T(8,128)(2,1)S(1)}, bf16[2,256,2,256]{1,3,2,0:T(8,128)(2,1)}, u32[]{:S(2)}) copy-start(bf16[2,256,2,256]{1,3,2,0:T(8,128)(2,1)} %get-tuple-element.58) | copy-start | bytes 1572868
  163.4 3.4 %collective-permute-start.7 = (bf16[256,512]{1,0:T(8,128)(2,1)S(1)}, bf16[256,512]{1,0:T(8,128)(2,1)S(1)}, u32[]{:S(2)}, u32[]{:S(2)}) collective-permute-start(bf16[256,512]{1,0:T(8,128)(2,1)S(1)} %add_convert_fusion.5), channel_id=1, source_target_pairs={{1,0},{4,1},{5,4},{8,5},{9,8},{12,9},{13,12},{3,2},{6,3},{7,6},{10... | collective-permute-start | bytes 786440 | tf_op jit(solution)/shard_map/ppermute | solution.py:14
  164.7 5.3 %copy-start.2 = (f32[2,32,8,256]{3,2,0,1:T(8,128)S(1)}, f32[2,32,8,256]{3,2,0,1:T(8,128)}, u32[]{:S(2)}) copy-start(f32[2,32,8,256]{3,2,0,1:T(8,128)} %copy-done.1) | copy-start | bytes 1572868
  164.7 5.3 %copy-start.4 = (bf16[256,512]{1,0:T(8,128)(2,1)S(1)}, bf16[256,512]{1,0:T(8,128)(2,1)}, u32[]{:S(2)}) copy-start(bf16[256,512]{1,0:T(8,128)(2,1)} %copy-done.3) | copy-start | bytes 786436
  167.6 7.7 %collective-permute-start.8 = (bf16[256,512]{1,0:T(8,128)(2,1)}, bf16[256,512]{1,0:T(8,128)(2,1)}, u32[]{:S(2)}, u32[]{:S(2)}) collective-permute-start(bf16[256,512]{1,0:T(8,128)(2,1)} %add_convert_fusion.4), channel_id=1, source_target_pairs={{1,0},{4,1},{5,4},{8,5},{9,8},{12,9},{13,12},{3,2},{6,3},{7,6},{10... | collective-permute-start | bytes 786440 | tf_op jit(solution)/shard_map/ppermute | solution.py:14
Sparse Core Ops, SparseCore 0:
  99.3 39.3 reduce-scatter.3
  141.7 19.8 all-reduce.2
  164.0 59.8 all-reduce.4
